TPU v7x, 256 devices: a whole 4x4x8 slice. The times are simulated.
256 devices in a mesh: section: 32 (over z_hi, y, core), tensor: 8 (over z_lo, x).
Axes of the slice: x: 4, y: 4, z: 8 (z_hi: 4, z_lo: 2; z = z_hi * 2 + z_lo), core: 2. Of those that a mesh axis runs over, the one named last changes fastest.
Arguments:
- acts: bfloat16 [32, 512, 3072], P('section', 'tensor'), may hold values from -6 to 6
- sides: bfloat16 [32, 512, 3072], P('section', 'tensor'), may hold values from -6 to 6
- gains: float32 [32, 3072], P('section'), may hold values from 0.1 to 1.9
- weights: bfloat16 [32, 6144, 3072], P('section', None, 'tensor'), may hold values from -0.078125 to 0.078125
- back_acts: bfloat16 [32, 512, 3072], P('section', 'tensor'), may hold values from -6 to 6
- back_sides: bfloat16 [32, 512, 3072], P('section', 'tensor'), may hold values from -6 to 6
- back_grads: bfloat16 [32, 512, 3072], P('section', 'tensor'), may hold values from -6 to 6
Outputs:
- received: bfloat16 [32, 512, 3072], P('section', 'tensor')
- mirrored: bfloat16 [32, 512, 3072], P('section', 'tensor')
- grad_received: bfloat16 [32, 512, 3072], P('section', 'tensor')
- weight_grads: bfloat16 [32, 6144, 3072], P('section', None, 'tensor')
- gain_grads: float32 [32, 3072], P('section')
All inputs are finite; a program needn't handle non-finite values.
Results may differ from a plain program's by a relative error of at most 0.015.
Values may be sent and summed in bfloat16 or wider, within the bound.
No kernel may reach another device: no remote copies, remote signals or barrier semaphores. Data moves between devices by JAX's collectives and lax.ppermute only.
A program may use at most 128 MiB of HBM per device.

v0:
```python
import jax
import jax.numpy as jnp
from jax import lax
from jax.sharding import PartitionSpec as P

epsilon = 1e-06
tanh_scale = 0.7978845608028654
cubic_term = 0.044715


def swapped(block, axis, apart):
    count = lax.axis_size(axis)
    route = []
    for low in range(count):
        high = low | 1 << apart
        if high != low and high < count:
            route += [(low, high), (high, low)]
    return lax.ppermute(block, axis, route)


def shifted(block, axis, distance):
    devices = range(lax.axis_size(axis))
    route = [((i - distance) % len(devices), i) for i in devices]
    return lax.ppermute(block, axis, route)


def gelu_value(inputs):
    inside = tanh_scale * (inputs + cubic_term * inputs * inputs * inputs)
    return 0.5 * inputs * (1.0 + jnp.tanh(inside))


def gelu_slope(inputs):
    inside = tanh_scale * (inputs + cubic_term * inputs * inputs * inputs)
    bent = jnp.tanh(inside)
    return 0.5 * (1.0 + bent) + 0.5 * inputs * (1.0 - bent * bent) * tanh_scale * (
        1.0 + 3.0 * cubic_term * inputs * inputs
    )


def normalize(rows_in, gain):
    xfloat = rows_in.astype(jnp.float32)
    rinv = lax.rsqrt(jnp.mean(xfloat * xfloat, axis=-1, keepdims=True) + epsilon)
    return (xfloat, rinv, (xfloat * rinv * gain).astype(jnp.bfloat16))


def mirror(payload):
    sections = lax.axis_size("section")
    levels = sections.bit_length() - 1
    for bit_idx in range(levels):
        payload = swapped(payload, "section", bit_idx)
    return payload


def on_device(acts, sides, gains, weights, back_acts, back_sides, back_grads):
    sections = lax.axis_size("section")
    middle = sections // 2
    section_idx = lax.axis_index("section")
    gain = gains[0]
    weight_all = weights[0]
    rows, width = acts[0].shape
    w_top = weight_all[:width]
    w_bottom = weight_all[width:]
    xfloat, rinv, normed = normalize(acts[0], gain)
    normed_all, side_all = (
        lax.all_gather(normed, "tensor", axis=0, tiled=True),
        lax.all_gather(sides[0], "tensor", axis=0, tiled=True),
    )
    hidden = jnp.dot(normed_all, w_top, preferred_element_type=jnp.float32) + jnp.dot(
        side_all, w_bottom, preferred_element_type=jnp.float32
    )
    update = lax.all_to_all(
        gelu_value(hidden).astype(jnp.bfloat16), "tensor", split_axis=0, concat_axis=1, tiled=True
    ).astype(jnp.float32)
    out_rows = (xfloat + update).astype(jnp.bfloat16)
    received = shifted(out_rows, "section", 1)
    bfloat, brinv, bnormed = normalize(back_acts[0], gain)
    bnormed_all, bside_all = (
        lax.all_gather(bnormed, "tensor", axis=0, tiled=True),
        lax.all_gather(back_sides[0], "tensor", axis=0, tiled=True),
    )
    bhidden = jnp.dot(bnormed_all, w_top, preferred_element_type=jnp.float32) + jnp.dot(
        bside_all, w_bottom, preferred_element_type=jnp.float32
    )
    grad_cols = lax.all_to_all(back_grads[0], "tensor", split_axis=1, concat_axis=0, tiled=True)
    dhidden = (grad_cols.astype(jnp.float32) * gelu_slope(bhidden)).astype(jnp.bfloat16)
    contract = (((0,), (0,)), ((), ()))
    grad_top = lax.dot_general(bnormed_all, dhidden, contract, preferred_element_type=jnp.float32)
    grad_bottom = lax.dot_general(bside_all, dhidden, contract, preferred_element_type=jnp.float32)
    weight_grads = jnp.concatenate([grad_top, grad_bottom], axis=0).astype(jnp.bfloat16)
    across = (((1,), (1,)), ((), ()))
    dfused = lax.psum_scatter(
        lax.dot_general(dhidden, weight_all, across, preferred_element_type=jnp.float32).astype(
            jnp.bfloat16
        ),
        "tensor",
        scatter_dimension=0,
        tiled=True,
    ).astype(jnp.float32)
    dnormed = dfused[:, :width]
    dside = dfused[:, width:].astype(jnp.bfloat16)
    gain_part = jnp.sum(dnormed * bfloat * brinv, axis=0)
    gain_grad = lax.psum(gain_part, "tensor")
    scaled = gain * dnormed
    dnorm_in = brinv * scaled - bfloat * brinv * brinv * brinv * jnp.mean(
        scaled * bfloat, axis=-1, keepdims=True
    )
    dx_rows = (back_grads[0].astype(jnp.float32) + dnorm_in).astype(jnp.bfloat16)
    grad_received = shifted(dx_rows, "section", -1)
    payload = jnp.where(section_idx < middle, out_rows, dside)
    mirrored = mirror(payload)
    return (
        received[None],
        mirrored[None],
        grad_received[None],
        weight_grads[None],
        gain_grad[None],
    )


def solution(mesh):
    placed = (
        P("section", "tensor", None),
        P("section", "tensor", None),
        P("section", None),
        P("section", None, "tensor"),
        P("section", "tensor", None),
        P("section", "tensor", None),
        P("section", "tensor", None),
    )
    return jax.shard_map(
        on_device,
        mesh=mesh,
        in_specs=placed,
        out_specs=(
            P("section", "tensor", None),
            P("section", "tensor", None),
            P("section", "tensor", None),
            P("section", None, "tensor"),
            P("section", None),
        ),
        check_vma=False,
    )
```

profile of v0, /device:TPU:24, one launch (start us, length us, event | category | flops | bytes accessed | tf_op | source)
XLA Modules:
  0.0 420.0 jit_solution(7512101617935437952)
XLA Ops:
  7.2 0.0 all-gather.9.cloned.1.call-start
  7.2 1.2 fusion.53
  8.4 1.9 fusion.31
  10.3 0.0 all-gather.13.cloned.1.call-start
  10.4 0.7 all-gather.13.cloned.1.call-update
  11.1 1.0 copy.17
  12.1 0.8 copy.13
  12.9 5.7 %all-to-all-start.1 = ((bf16[64,8,384]{2,0,1:T(8,128)(2,1)}), bf16[64,8,384]{2,0,1:T(8,128)(2,1)S(1)}, u32[]{:S(2)}, u32[]{:S(2)}) async-start(bf16[64,8,384]{2,0,1:T(8,128)(2,1)} %copy.13), calls=%async_computation.1 | async-start | bytes 786432 | tf_op jit(solution)/shard_map/all_to_all | solution.py:84
  18.6 41.1 %all-gather.9.cloned.1.call-done = bf16[512,3072]{1,0:T(8,128)(2,1)} async-done(((bf16[64,3072]{1,0:T(8,128)(2,1)}), bf16[512,3072]{1,0:T(8,128)(2,1)}) %all-gather.9.cloned.1.call-update) | async-done | bytes 3145744 | tf_op jit(solution)/shard_map/all_gather | solution.py:78
  59.7 4.4 %fusion.10 = f32[512,384]{1,0:T(8,128)S(1)} fusion(bf16[512,3072]{1,0:T(8,128)(2,1)} %all-gather.9.cloned.1.call-done, bf16[1,6144,384]{2,1,0:T(8,128)(2,1)} %param.10), kind=kOutput, calls=%fused_computation.14 | convolution fusion | flops 1207959552 | bytes 6291456 | tf_op jit(solution)/shard_map/dot_general | solution.py:81
  64.1 43.7 %all-gather.13.cloned.1.call-done = bf16[1,512,3072]{2,1,0:T(8,128)(2,1)} async-done(((bf16[1,64,3072]{2,1,0:T(8,128)(2,1)}), bf16[1,512,3072]{2,1,0:T(8,128)(2,1)}) %all-gather.13.cloned.1.call-update) | async-done | bytes 3145744 | tf_op jit(solution)/shard_map/all_gather | solution.py:79
  107.9 4.9 %fusion.48 = bf16[512,384]{1,0:T(8,128)(2,1)S(1)} fusion(f32[512,384]{1,0:T(8,128)S(1)} %fusion.10, bf16[1,6144,384]{2,1,0:T(8,128)(2,1)} %param.10, bf16[1,512,3072]{2,1,0:T(8,128)(2,1)} %all-gather.13.cloned.1.call-done, bf16[64,8,384]{2,0,1:T(8,128)(2,1)S(1)} %all-to-all-done.1), kind=kOutput, calls=%fused_computation.55 | convolution fusion | flops 1212088320 | bytes 7077888 | tf_op jit(solution)/shard_map/dot_general | solution.py:81
  112.7 7.8 %convolution_convert_fusion = bf16[512,6144]{1,0:T(8,128)(2,1)} fusion(bf16[512,384]{1,0:T(8,128)(2,1)S(1)} %fusion.48, bf16[1,6144,384]{2,1,0:T(8,128)(2,1)} %param.10), kind=kOutput, calls=%fused_computation | convolution fusion | flops 2419064832 | bytes 11403264 | tf_op jit(solution)/shard_map/dot_general | solution.py:92
  120.5 0.0 all-gather.7.cloned.1.call-start
  120.6 0.9 copy-done.1
  121.5 0.2 fusion.49
  121.7 74.3 %reduce-scatter.2.cloned.1.call-done = bf16[64,6144]{1,0:T(8,128)(2,1)} async-done(((bf16[512,6144]{1,0:T(8,128)(2,1)}), bf16[64,6144]{1,0:T(8,128)(2,1)}) %reduce-scatter.2.cloned.1.call-update) | async-done | bytes 786448 | tf_op jit(solution)/shard_map/reduce_scatter | solution.py:91
  196.0 1.3 fusion.56
  197.3 2.2 fusion.36
  199.5 0.0 all-gather.11.cloned.1.call-start
  199.6 0.5 all-gather.11.cloned.1.call-update
  200.1 44.9 %all-gather.7.cloned.1.call-done = bf16[512,3072]{1,0:T(8,128)(2,1)} async-done(((bf16[64,3072]{1,0:T(8,128)(2,1)}), bf16[512,3072]{1,0:T(8,128)(2,1)}) %all-gather.7.cloned.1.call-update) | async-done | bytes 3145744 | tf_op jit(solution)/shard_map/all_gather | solution.py:65
  245.0 4.4 %fusion.12 = f32[512,384]{1,0:T(8,128)S(1)} fusion(bf16[512,3072]{1,0:T(8,128)(2,1)} %all-gather.7.cloned.1.call-done, bf16[1,6144,384]{2,1,0:T(8,128)(2,1)} %param.10), kind=kOutput, calls=%fused_computation.16 | convolution fusion | flops 1207959552 | bytes 6291456 | tf_op jit(solution)/shard_map/dot_general | solution.py:68
  249.4 43.6 %all-gather.11.cloned.1.call-done = bf16[1,512,3072]{2,1,0:T(8,128)(2,1)} async-done(((bf16[1,64,3072]{2,1,0:T(8,128)(2,1)}), bf16[1,512,3072]{2,1,0:T(8,128)(2,1)}) %all-gather.11.cloned.1.call-update) | async-done | bytes 3145744 | tf_op jit(solution)/shard_map/all_gather | solution.py:66
  293.0 5.3 %fusion.41 = bf16[512,384]{1,0:T(8,128)(2,1)} fusion(f32[512,384]{1,0:T(8,128)S(1)} %fusion.12, bf16[1,6144,384]{2,1,0:T(8,128)(2,1)} %param.10, bf16[1,512,3072]{2,1,0:T(8,128)(2,1)} %all-gather.11.cloned.1.call-done), kind=kOutput, calls=%fused_computation.48 | convolution fusion | flops 1209925632 | bytes 6684672 | tf_op jit(solution)/shard_map/dot_general | solution.py:68
  298.3 3.8 all-to-all-start
  302.1 7.8 %all-to-all-done = bf16[8,64,384]{2,1,0:T(8,128)(2,1)S(1)} async-done(((bf16[8,64,384]{2,1,0:T(8,128)(2,1)}), bf16[8,64,384]{2,1,0:T(8,128)(2,1)S(1)}, u32[]{:S(2)}, u32[]{:S(2)}) %all-to-all-start) | async-done | bytes 393248 | tf_op jit(solution)/shard_map/all_to_all | solution.py:71
  309.9 0.1 convert_bitcast_fusion
  310.0 0.1 copy.16
  310.0 0.2 slice_select_fusion
  310.2 0.1 collective-permute-start.1
  310.3 1.7 collective-permute-done.1
  312.0 0.8 collective-permute-start.2
  312.8 10.3 %collective-permute-done.2 = bf16[64,3072]{1,0:T(8,128)(2,1)S(1)} collective-permute-done((bf16[64,3072]{1,0:T(8,128)(2,1)S(1)}, bf16[64,3072]{1,0:T(8,128)(2,1)S(1)}, u32[]{:S(2)}, u32[]{:S(2)}) %collective-permute-start.2) | collective-permute-done | bytes 393248 | tf_op jit(solution)/shard_map/ppermute | solution.py:18
  323.2 1.4 collective-permute-start.3
  324.6 10.4 %collective-permute-done.3 = bf16[64,3072]{1,0:T(8,128)(2,1)S(1)} collective-permute-done((bf16[64,3072]{1,0:T(8,128)(2,1)S(1)}, bf16[64,3072]{1,0:T(8,128)(2,1)S(1)}, u32[]{:S(2)}, u32[]{:S(2)}) %collective-permute-start.3) | collective-permute-done | bytes 393248 | tf_op jit(solution)/shard_map/ppermute | solution.py:18
  335.0 2.5 collective-permute-start.4
  337.5 1.9 fusion.2
  339.4 1.9 fusion.1
  341.3 0.1 collective-permute-start.6
  341.3 0.5 collective-permute-start
  341.8 11.9 %collective-permute-done.4 = bf16[64,3072]{1,0:T(8,128)(2,1)S(1)} collective-permute-done((bf16[64,3072]{1,0:T(8,128)(2,1)S(1)}, bf16[64,3072]{1,0:T(8,128)(2,1)S(1)}, u32[]{:S(2)}, u32[]{:S(2)}) %collective-permute-start.4) | collective-permute-done | bytes 393248 | tf_op jit(solution)/shard_map/ppermute | solution.py:18
  353.7 4.8 %collective-permute-start.5 = (bf16[64,3072]{1,0:T(8,128)(2,1)S(1)}, bf16[64,3072]{1,0:T(8,128)(2,1)S(1)}, u32[]{:S(2)}, u32[]{:S(2)}) collective-permute-start(bf16[64,3072]{1,0:T(8,128)(2,1)S(1)} %collective-permute-done.4), channel_id=1, source_target_pairs={{0,128},{128,0},{8,136},{136,8},{16,144},{144,16},{24,152},{152,24... | collective-permute-start | bytes 1179656 | tf_op jit(solution)/shard_map/ppermute | solution.py:18
  358.6 2.7 pad_maximum_fusion
  361.2 50.0 %psum.7 = f32[1,3072]{1,0:T(1,128)} all-reduce(f32[1,3072]{1,0:T(1,128)S(1)} %bitcast.91), channel_id=1, replica_groups=mesh['section'=32,'tensor'=8] {'tensor'}, use_global_device_ids=true, to_apply=%region_5.0 | all-reduce | flops 3072 | bytes 24576 | tf_op jit(solution)/shard_map/psum | solution.py:102
  411.2 0.7 copy.21
  412.0 0.7 copy.22
  412.7 0.7 copy.23
  (24 shorter events, 0.1 us)
Async XLA Ops:
  7.2 52.6 %all-gather.9.cloned.1.call-start = ((), (), s32[]{:S(2)}) async-start(), calls=%async_computation.4 | async-start | bytes 3538944 | tf_op jit(solution)/shard_map/all_gather | solution.py:78
  10.3 97.5 %all-gather.13.cloned.1.call-start = ((), (), s32[]{:S(2)}) async-start(), calls=%async_computation.7 | async-start | bytes 3538944 | tf_op jit(solution)/shard_map/all_gather | solution.py:79
  12.9 51.2 %all-to-all-start.1 = ((bf16[64,8,384]{2,0,1:T(8,128)(2,1)}), bf16[64,8,384]{2,0,1:T(8,128)(2,1)S(1)}, u32[]{:S(2)}, u32[]{:S(2)}) async-start(bf16[64,8,384]{2,0,1:T(8,128)(2,1)} %copy.13), calls=%async_computation.1 | async-start | bytes 786432 | tf_op jit(solution)/shard_map/all_to_all | solution.py:84
  18.6 177.4 %reduce-scatter.2.cloned.1.call-start = ((), (), s32[]{:S(2)}) async-start(), calls=%async_computation.5 | async-start | bytes 7077888 | tf_op jit(solution)/shard_map/reduce_scatter | solution.py:91
  120.5 1.0 copy-start.1
  120.5 75.5 %copy-start = (bf16[1,64,3072]{2,1,0:T(8,128)(2,1)S(1)}, bf16[1,64,3072]{2,1,0:T(8,128)(2,1)}, u32[]{:S(2)}) copy-start(bf16[1,64,3072]{2,1,0:T(8,128)(2,1)} %param.11) | copy-start | bytes 1179652
  120.5 75.5 %copy-start.4 = (f32[1,3072]{1,0:T(1,128)S(1)}, f32[1,3072]{1,0:T(1,128)}, u32[]{:S(2)}) copy-start(f32[1,3072]{1,0:T(1,128)} %param.9) | copy-start | bytes 36868
  120.5 76.8 %copy-start.3 = (bf16[1,64,3072]{2,1,0:T(8,128)(2,1)S(1)}, bf16[1,64,3072]{2,1,0:T(8,128)(2,1)}, u32[]{:S(2)}) copy-start(bf16[1,64,3072]{2,1,0:T(8,128)(2,1)} %param.13) | copy-start | bytes 1179652
  120.5 124.5 %all-gather.7.cloned.1.call-start = ((), (), s32[]{:S(2)}) async-start(), calls=%async_computation.3 | async-start | bytes 3538944 | tf_op jit(solution)/shard_map/all_gather | solution.py:65
  199.5 93.4 %all-gather.11.cloned.1.call-start = ((), (), s32[]{:S(2)}) async-start(), calls=%async_computation.6 | async-start | bytes 3538944 | tf_op jit(solution)/shard_map/all_gather | solution.py:66
  298.3 11.7 %copy-start.2 = (bf16[64,6144]{1,0:T(8,128)(2,1)S(1)}, bf16[64,6144]{1,0:T(8,128)(2,1)}, u32[]{:S(2)}) copy-start(bf16[64,6144]{1,0:T(8,128)(2,1)} %reduce-scatter.2.cloned.1.call-done) | copy-start | bytes 2359300
  298.3 11.6 %all-to-all-start = ((bf16[8,64,384]{2,1,0:T(8,128)(2,1)}), bf16[8,64,384]{2,1,0:T(8,128)(2,1)S(1)}, u32[]{:S(2)}, u32[]{:S(2)}) async-start(bf16[8,64,384]{2,1,0:T(8,128)(2,1)} %bitcast.6), calls=%async_computation | async-start | bytes 786432 | tf_op jit(solution)/shard_map/all_to_all | solution.py:71
  309.9 27.6 %copy-start.6 = (bf16[1,512,3072]{2,1,0:T(8,128)(2,1)S(1)}, bf16[1,512,3072]{2,1,0:T(8,128)(2,1)}, u32[]{:S(2)}) copy-start(bf16[1,512,3072]{2,1,0:T(8,128)(2,1)} %all-gather.13.cloned.1.call-done) | copy-start | bytes 9437188
  310.2 29.2 %copy-start.5 = (bf16[512,3072]{1,0:T(8,128)(2,1)S(1)}, bf16[512,3072]{1,0:T(8,128)(2,1)}, u32[]{:S(2)}) copy-start(bf16[512,3072]{1,0:T(8,128)(2,1)} %all-gather.9.cloned.1.call-done) | copy-start | bytes 9437188
  310.2 1.8 collective-permute-start.1
  312.0 11.2 %collective-permute-start.2 = (bf16[64,3072]{1,0:T(8,128)(2,1)S(1)}, bf16[64,3072]{1,0:T(8,128)(2,1)S(1)}, u32[]{:S(2)}, u32[]{:S(2)}) collective-permute-start(bf16[64,3072]{1,0:T(8,128)(2,1)S(1)} %collective-permute-done.1), channel_id=1, source_target_pairs={{0,16},{16,0},{8,24},{24,8},{32,48},{48,32},{40,56},{56,40},{64,80... | collective-permute-start | bytes 1179656 | tf_op jit(solution)/shard_map/ppermute | solution.py:18
  323.2 11.8 %collective-permute-start.3 = (bf16[64,3072]{1,0:T(8,128)(2,1)S(1)}, bf16[64,3072]{1,0:T(8,128)(2,1)S(1)}, u32[]{:S(2)}, u32[]{:S(2)}) collective-permute-start(bf16[64,3072]{1,0:T(8,128)(2,1)S(1)} %collective-permute-done.2), channel_id=1, source_target_pairs={{0,32},{32,0},{8,40},{40,8},{16,48},{48,16},{24,56},{56,24},{64,96... | collective-permute-start | bytes 1179656 | tf_op jit(solution)/shard_map/ppermute | solution.py:18
  335.0 18.8 %collective-permute-start.4 = (bf16[64,3072]{1,0:T(8,128)(2,1)S(1)}, bf16[64,3072]{1,0:T(8,128)(2,1)S(1)}, u32[]{:S(2)}, u32[]{:S(2)}) collective-permute-start(bf16[64,3072]{1,0:T(8,128)(2,1)S(1)} %collective-permute-done.3), channel_id=1, source_target_pairs={{0,64},{64,0},{8,72},{72,8},{16,80},{80,16},{24,88},{88,24},{32,96... | collective-permute-start | bytes 1179656 | tf_op jit(solution)/shard_map/ppermute | solution.py:18
  341.3 70.0 %collective-permute-start.6 = (bf16[64,3072]{1,0:T(8,128)(2,1)S(1)}, bf16[64,3072]{1,0:T(8,128)(2,1)S(1)}, u32[]{:S(2)}, u32[]{:S(2)}) collective-permute-start(bf16[64,3072]{1,0:T(8,128)(2,1)S(1)} %get-tuple-element.9), channel_id=1, source_target_pairs={{8,0},{16,8},{24,16},{32,24},{40,32},{48,40},{56,48},{64,56},{72,6... | collective-permute-start | bytes 1179656 | tf_op jit(solution)/shard_map/ppermute | solution.py:24
  341.3 69.9 %collective-permute-start = (bf16[64,3072]{1,0:T(8,128)(2,1)S(1)}, bf16[64,3072]{1,0:T(8,128)(2,1)S(1)}, u32[]{:S(2)}, u32[]{:S(2)}) collective-permute-start(bf16[64,3072]{1,0:T(8,128)(2,1)S(1)} %get-tuple-element.8), channel_id=1, source_target_pairs={{248,0},{0,8},{8,16},{16,24},{24,32},{32,40},{40,48},{48,56},{56,6... | collective-permute-start | bytes 1179656 | tf_op jit(solution)/shard_map/ppermute | solution.py:24
  353.7 57.5 %collective-permute-start.5 = (bf16[64,3072]{1,0:T(8,128)(2,1)S(1)}, bf16[64,3072]{1,0:T(8,128)(2,1)S(1)}, u32[]{:S(2)}, u32[]{:S(2)}) collective-permute-start(bf16[64,3072]{1,0:T(8,128)(2,1)S(1)} %collective-permute-done.4), channel_id=1, source_target_pairs={{0,128},{128,0},{8,136},{136,8},{16,144},{144,16},{24,152},{152,24... | collective-permute-start | bytes 1179656 | tf_op jit(solution)/shard_map/ppermute | solution.py:18
Sparse Core Ops, SparseCore 0:
  10.5 49.2 all-gather.8
  61.5 46.2 all-gather.12
  120.7 75.2 reduce-scatter.1
  199.6 45.3 all-gather.6
  246.6 46.2 all-gather.10
where the time goes:
time: 421 us; the launch traced here: 420 us
  waiting for transfers between devices  291 us (69%)
  blocking collectives  50 us (12%)
  matrix products  30.5 us (7%)
  starting transfers between devices  20 us (5%)
  between operations  13.9 us (3%)
  other arithmetic  9.67 us (2%)
  local copies, waits for them, and re-layouts  5.07 us (1%)
    reduce_scatter x1, waiting for transfers between devices, on_device(): lax.psum_scatter(lax.dot_general(dhidden, weight_all, across, preferred_e...  74.3 us
    psum x1, blocking collectives, on_device(): gain_grad = lax.psum(gain_part, 'tensor')  50 us
    all_gather x1, waiting for transfers between devices, on_device(): lax.all_gather(normed, 'tensor', axis=0, tiled=True)  44.9 us
    all_gather x1, waiting for transfers between devices, on_device(): lax.all_gather(back_sides[0], 'tensor', axis=0, tiled=True)  43.7 us
    all_gather x1, waiting for transfers between devices, on_device(): lax.all_gather(sides[0], 'tensor', axis=0, tiled=True)  43.6 us
    all_gather x1, waiting for transfers between devices, on_device(): lax.all_gather(bnormed, 'tensor', axis=0, tiled=True)  41.1 us
    ppermute x5, waiting for transfers between devices, swapped(): return lax.ppermute(block, axis, route)  34.3 us
    ppermute x5, starting transfers between devices, swapped(): return lax.ppermute(block, axis, route)  9.73 us
  transfers between devices with their start and end apart: 14, of which 10 were waited for; matrix products, arithmetic and copies ran while one was open for 4% of the time, Pallas kernels for 0%

commit v1 on v0

--- a/solution.py
+++ b/solution.py
@@ -76,7 +76,10 @@
     bfloat, brinv, bnormed = normalize(back_acts[0], gain)
     bnormed_all, bside_all = (
         lax.all_gather(bnormed, "tensor", axis=0, tiled=True),
-        lax.all_gather(back_sides[0], "tensor", axis=0, tiled=True),
+        jnp.concatenate(
+            lax.all_to_all(jnp.stack([back_sides[0]] * lax.axis_size("tensor")), "tensor", 0, 0),
+            axis=0,
+        ),
     )
     bhidden = jnp.dot(bnormed_all, w_top, preferred_element_type=jnp.float32) + jnp.dot(
         bside_all, w_bottom, preferred_element_type=jnp.float32

time: 421 us -> 403 us (0.957)
  waiting for transfers between devices: 291 us -> 267 us
  starting transfers between devices: 20 us -> 24.8 us
    all_to_all x0 -> x1, waiting for transfers between devices: none -> 48.2 us  [on_device(): lax.all_to_all(jnp.stack([back_sides[0]] * lax.axis_size('tensor')), 'ten...]
    all_gather x1 -> x0, waiting for transfers between devices: 43.7 us -> none  [on_device(): lax.all_gather(back_sides[0], 'tensor', axis=0, tiled=True)]
    all_gather x1, waiting for transfers between devices: 41.1 us -> 4.79 us  [on_device(): lax.all_gather(bnormed, 'tensor', axis=0, tiled=True)]
    all_to_all x1, waiting for transfers between devices: 0.01 us -> 8.85 us  [on_device(): lax.all_to_all(back_grads[0], 'tensor', split_axis=1, concat_axis=0, tile...]
    all_to_all x0 -> x1, starting transfers between devices: none -> 5.79 us  [on_device(): lax.all_to_all(jnp.stack([back_sides[0]] * lax.axis_size('tensor')), 'ten...]
  transfers between devices with their start and end apart: 14 -> 14, of which waited for: 10 -> 11; matrix products, arithmetic and copies ran while one was open for 4% -> 5% of each run, Pallas kernels for 0% -> 0%
where the time goes in v1:
time: 403 us; the launch traced here: 402 us
  waiting for transfers between devices  267 us (66%)
  blocking collectives  49.8 us (12%)
  matrix products  32.4 us (8%)
  starting transfers between devices  24.8 us (6%)
  between operations  13.9 us (3%)
  other arithmetic  7.68 us (2%)
  local copies, waits for them, and re-layouts  7.12 us (2%)
    reduce_scatter x1, waiting for transfers between devices, on_device(): lax.psum_scatter(lax.dot_general(dhidden, weight_all, across, preferred_e...  75.4 us
    psum x1, blocking collectives, on_device(): gain_grad = lax.psum(gain_part, 'tensor')  49.8 us
    all_to_all x1, waiting for transfers between devices, on_device(): lax.all_to_all(jnp.stack([back_sides[0]] * lax.axis_size('tensor')), 'ten...  48.2 us
    all_gather x1, waiting for transfers between devices, on_device(): lax.all_gather(normed, 'tensor', axis=0, tiled=True)  44.9 us
    all_gather x1, waiting for transfers between devices, on_device(): lax.all_gather(sides[0], 'tensor', axis=0, tiled=True)  43.6 us
    ppermute x5, waiting for transfers between devices, swapped(): return lax.ppermute(block, axis, route)  32.4 us
    ppermute x5, starting transfers between devices, swapped(): return lax.ppermute(block, axis, route)  9.73 us
    all_to_all x1, waiting for transfers between devices, on_device(): lax.all_to_all(back_grads[0], 'tensor', split_axis=1, concat_axis=0, tile...  8.85 us
  transfers between devices with their start and end apart: 14, of which 11 were waited for; matrix products, arithmetic and copies ran while one was open for 5% of the time, Pallas kernels for 0%

profile of v1, /device:TPU:24, one launch (start us, length us, event | category | flops | bytes accessed | tf_op | source)
XLA Modules:
  0.0 402.3 jit_solution(692399063254372523)
XLA Ops:
  7.2 3.0 stack.3
  10.2 5.8 %all-to-all-start.2 = ((bf16[8,64,3072]{2,1,0:T(8,128)(2,1)}), bf16[8,64,3072]{2,1,0:T(8,128)(2,1)}, u32[]{:S(2)}, u32[]{:S(2)}) async-start(bf16[8,64,3072]{2,1,0:T(8,128)(2,1)} %stack.3), calls=%async_computation.2 | async-start | bytes 6291456 | tf_op jit(solution)/shard_map/all_to_all | solution.py:80
  16.1 0.2 fusion.49
  16.3 0.9 fusion.27
  17.3 0.8 copy.13
  18.0 48.2 %all-to-all-done.2 = bf16[8,64,3072]{2,1,0:T(8,128)(2,1)} async-done(((bf16[8,64,3072]{2,1,0:T(8,128)(2,1)}), bf16[8,64,3072]{2,1,0:T(8,128)(2,1)}, u32[]{:S(2)}, u32[]{:S(2)}) %all-to-all-start.2) | async-done | bytes 3145760 | tf_op jit(solution)/shard_map/all_to_all | solution.py:80
  66.3 4.8 %all-to-all-start.1 = ((bf16[64,8,384]{2,0,1:T(8,128)(2,1)}), bf16[64,8,384]{2,0,1:T(8,128)(2,1)S(1)}, u32[]{:S(2)}, u32[]{:S(2)}) async-start(bf16[64,8,384]{2,0,1:T(8,128)(2,1)} %copy.13), calls=%async_computation.1 | async-start | bytes 786432 | tf_op jit(solution)/shard_map/all_to_all | solution.py:87
  71.0 0.0 reduce-scatter.2.cloned.1.call-start
  71.1 4.5 %fusion.5 = f32[512,384]{1,0:T(8,128)S(1)} fusion(bf16[512,3072]{1,0:T(8,128)(2,1)} %bitcast.14, bf16[1,6144,384]{2,1,0:T(8,128)(2,1)} %param.10), kind=kOutput, calls=%fused_computation.9 | convolution fusion | flops 1207959552 | bytes 6291456 | tf_op jit(solution)/shard_map/dot_general | solution.py:84
  75.6 8.9 %all-to-all-done.1 = bf16[64,8,384]{2,0,1:T(8,128)(2,1)S(1)} async-done(((bf16[64,8,384]{2,0,1:T(8,128)(2,1)}), bf16[64,8,384]{2,0,1:T(8,128)(2,1)S(1)}, u32[]{:S(2)}, u32[]{:S(2)}) %all-to-all-start.1) | async-done | bytes 393248 | tf_op jit(solution)/shard_map/all_to_all | solution.py:87
  84.4 4.8 %all-gather.7.cloned.1.call-done = bf16[512,3072]{1,0:T(8,128)(2,1)} async-done(((bf16[64,3072]{1,0:T(8,128)(2,1)}), bf16[512,3072]{1,0:T(8,128)(2,1)}) %all-gather.7.cloned.1.call-update) | async-done | bytes 3145744 | tf_op jit(solution)/shard_map/all_gather | solution.py:78
  89.2 4.9 %fusion.44 = bf16[512,384]{1,0:T(8,128)(2,1)S(1)} fusion(f32[512,384]{1,0:T(8,128)S(1)} %fusion.5, bf16[512,3072]{1,0:T(8,128)(2,1)} %all-gather.7.cloned.1.call-done, bf16[1,6144,384]{2,1,0:T(8,128)(2,1)} %param.10, bf16[64,8,384]{2,0,1:T(8,128)(2,1)S(1)} %all-to-all-done.1), kind=kOutput, calls=%fused_computation.53 | convolution fusion | flops 1212088320 | bytes 7077888 | tf_op jit(solution)/shard_map/dot_general | solution.py:84
  94.1 7.8 %convolution_convert_fusion = bf16[512,6144]{1,0:T(8,128)(2,1)} fusion(bf16[512,384]{1,0:T(8,128)(2,1)S(1)} %fusion.44, bf16[1,6144,384]{2,1,0:T(8,128)(2,1)} %param.10), kind=kOutput, calls=%fused_computation | convolution fusion | flops 2419064832 | bytes 11403264 | tf_op jit(solution)/shard_map/dot_general | solution.py:95
  101.9 0.0 all-gather.5.cloned.1.call-start
  101.9 0.9 copy-done.1
  102.8 0.2 fusion.45
  103.0 75.4 %reduce-scatter.2.cloned.1.call-done = bf16[64,6144]{1,0:T(8,128)(2,1)} async-done(((bf16[512,6144]{1,0:T(8,128)(2,1)}), bf16[64,6144]{1,0:T(8,128)(2,1)}) %reduce-scatter.2.cloned.1.call-update) | async-done | bytes 786448 | tf_op jit(solution)/shard_map/reduce_scatter | solution.py:94
  178.5 1.3 fusion.52
  179.8 2.2 fusion.32
  182.0 0.0 all-gather.9.cloned.1.call-start
  182.1 0.5 all-gather.9.cloned.1.call-update
  182.6 44.9 %all-gather.5.cloned.1.call-done = bf16[512,3072]{1,0:T(8,128)(2,1)} async-done(((bf16[64,3072]{1,0:T(8,128)(2,1)}), bf16[512,3072]{1,0:T(8,128)(2,1)}) %all-gather.5.cloned.1.call-update) | async-done | bytes 3145744 | tf_op jit(solution)/shard_map/all_gather | solution.py:65
  227.5 4.4 %fusion.10 = f32[512,384]{1,0:T(8,128)S(1)} fusion(bf16[512,3072]{1,0:T(8,128)(2,1)} %all-gather.5.cloned.1.call-done, bf16[1,6144,384]{2,1,0:T(8,128)(2,1)} %param.10), kind=kOutput, calls=%fused_computation.14 | convolution fusion | flops 1207959552 | bytes 6291456 | tf_op jit(solution)/shard_map/dot_general | solution.py:68
  231.9 43.6 %all-gather.9.cloned.1.call-done = bf16[1,512,3072]{2,1,0:T(8,128)(2,1)} async-done(((bf16[1,64,3072]{2,1,0:T(8,128)(2,1)}), bf16[1,512,3072]{2,1,0:T(8,128)(2,1)}) %all-gather.9.cloned.1.call-update) | async-done | bytes 3145744 | tf_op jit(solution)/shard_map/all_gather | solution.py:66
  275.5 5.3 %fusion.37 = bf16[512,384]{1,0:T(8,128)(2,1)} fusion(f32[512,384]{1,0:T(8,128)S(1)} %fusion.10, bf16[1,6144,384]{2,1,0:T(8,128)(2,1)} %param.10, bf16[1,512,3072]{2,1,0:T(8,128)(2,1)} %all-gather.9.cloned.1.call-done), kind=kOutput, calls=%fused_computation.46 | convolution fusion | flops 1209925632 | bytes 6684672 | tf_op jit(solution)/shard_map/dot_general | solution.py:68
  280.8 3.8 all-to-all-start
  284.7 7.8 %all-to-all-done = bf16[8,64,384]{2,1,0:T(8,128)(2,1)S(1)} async-done(((bf16[8,64,384]{2,1,0:T(8,128)(2,1)}), bf16[8,64,384]{2,1,0:T(8,128)(2,1)S(1)}, u32[]{:S(2)}, u32[]{:S(2)}) %all-to-all-start) | async-done | bytes 393248 | tf_op jit(solution)/shard_map/all_to_all | solution.py:71
  292.4 0.1 convert_bitcast_fusion
  292.5 0.1 copy.16
  292.6 0.2 slice_select_fusion
  292.7 0.1 collective-permute-start.1
  292.8 1.7 collective-permute-done.1
  294.5 0.8 collective-permute-start.2
  295.4 10.3 %collective-permute-done.2 = bf16[64,3072]{1,0:T(8,128)(2,1)S(1)} collective-permute-done((bf16[64,3072]{1,0:T(8,128)(2,1)S(1)}, bf16[64,3072]{1,0:T(8,128)(2,1)S(1)}, u32[]{:S(2)}, u32[]{:S(2)}) %collective-permute-start.2) | collective-permute-done | bytes 393248 | tf_op jit(solution)/shard_map/ppermute | solution.py:18
  305.7 1.4 collective-permute-start.3
  307.1 10.4 %collective-permute-done.3 = bf16[64,3072]{1,0:T(8,128)(2,1)S(1)} collective-permute-done((bf16[64,3072]{1,0:T(8,128)(2,1)S(1)}, bf16[64,3072]{1,0:T(8,128)(2,1)S(1)}, u32[]{:S(2)}, u32[]{:S(2)}) %collective-permute-start.3) | collective-permute-done | bytes 393248 | tf_op jit(solution)/shard_map/ppermute | solution.py:18
  317.5 2.5 collective-permute-start.4
  320.1 3.7 fusion.2
  323.8 1.9 fusion.1
  325.7 0.1 collective-permute-start.6
  325.8 0.5 collective-permute-start
  326.3 10.0 %collective-permute-done.4 = bf16[64,3072]{1,0:T(8,128)(2,1)S(1)} collective-permute-done((bf16[64,3072]{1,0:T(8,128)(2,1)S(1)}, bf16[64,3072]{1,0:T(8,128)(2,1)S(1)}, u32[]{:S(2)}, u32[]{:S(2)}) %collective-permute-start.4) | collective-permute-done | bytes 393248 | tf_op jit(solution)/shard_map/ppermute | solution.py:18
  336.3 4.8 %collective-permute-start.5 = (bf16[64,3072]{1,0:T(8,128)(2,1)S(1)}, bf16[64,3072]{1,0:T(8,128)(2,1)S(1)}, u32[]{:S(2)}, u32[]{:S(2)}) collective-permute-start(bf16[64,3072]{1,0:T(8,128)(2,1)S(1)} %collective-permute-done.4), channel_id=1, source_target_pairs={{0,128},{128,0},{8,136},{136,8},{16,144},{144,16},{24,152},{152,24... | collective-permute-start | bytes 1179656 | tf_op jit(solution)/shard_map/ppermute | solution.py:18
  341.1 2.7 pad_maximum_fusion
  343.8 49.8 %psum.7 = f32[1,3072]{1,0:T(1,128)} all-reduce(f32[1,3072]{1,0:T(1,128)S(1)} %bitcast.87), channel_id=1, replica_groups=mesh['section'=32,'tensor'=8] {'tensor'}, use_global_device_ids=true, to_apply=%region_5.0 | all-reduce | flops 3072 | bytes 24576 | tf_op jit(solution)/shard_map/psum | solution.py:105
  393.5 0.7 copy.21
  394.3 0.7 copy.22
  395.0 0.7 copy.23
  (22 shorter events, 0.2 us)
Async XLA Ops:
  10.2 5.8 %copy-start = (bf16[1,64,3072]{2,1,0:T(8,128)(2,1)S(1)}, bf16[1,64,3072]{2,1,0:T(8,128)(2,1)}, u32[]{:S(2)}) copy-start(bf16[1,64,3072]{2,1,0:T(8,128)(2,1)} %param.11) | copy-start | bytes 1179652
  10.2 6.0 %copy-start.4 = (f32[1,3072]{1,0:T(1,128)S(1)}, f32[1,3072]{1,0:T(1,128)}, u32[]{:S(2)}) copy-start(f32[1,3072]{1,0:T(1,128)} %param.9) | copy-start | bytes 36868
  10.2 7.0 %copy-start.3 = (bf16[1,64,3072]{2,1,0:T(8,128)(2,1)S(1)}, bf16[1,64,3072]{2,1,0:T(8,128)(2,1)}, u32[]{:S(2)}) copy-start(bf16[1,64,3072]{2,1,0:T(8,128)(2,1)} %param.13) | copy-start | bytes 1179652
  10.2 56.1 %all-to-all-start.2 = ((bf16[8,64,3072]{2,1,0:T(8,128)(2,1)}), bf16[8,64,3072]{2,1,0:T(8,128)(2,1)}, u32[]{:S(2)}, u32[]{:S(2)}) async-start(bf16[8,64,3072]{2,1,0:T(8,128)(2,1)} %stack.3), calls=%async_computation.2 | async-start | bytes 6291456 | tf_op jit(solution)/shard_map/all_to_all | solution.py:80
  16.0 73.2 %all-gather.7.cloned.1.call-start = ((), (), s32[]{:S(2)}) async-start(), calls=%async_computation.5 | async-start | bytes 3538944 | tf_op jit(solution)/shard_map/all_gather | solution.py:78
  66.3 18.1 %all-to-all-start.1 = ((bf16[64,8,384]{2,0,1:T(8,128)(2,1)}), bf16[64,8,384]{2,0,1:T(8,128)(2,1)S(1)}, u32[]{:S(2)}, u32[]{:S(2)}) async-start(bf16[64,8,384]{2,0,1:T(8,128)(2,1)} %copy.13), calls=%async_computation.1 | async-start | bytes 786432 | tf_op jit(solution)/shard_map/all_to_all | solution.py:87
  71.0 107.4 %reduce-scatter.2.cloned.1.call-start = ((), (), s32[]{:S(2)}) async-start(), calls=%async_computation.6 | async-start | bytes 7077888 | tf_op jit(solution)/shard_map/reduce_scatter | solution.py:94
  101.8 1.0 copy-start.1
  101.9 125.6 %all-gather.5.cloned.1.call-start = ((), (), s32[]{:S(2)}) async-start(), calls=%async_computation.4 | async-start | bytes 3538944 | tf_op jit(solution)/shard_map/all_gather | solution.py:65
  182.0 93.5 %all-gather.9.cloned.1.call-start = ((), (), s32[]{:S(2)}) async-start(), calls=%async_computation.7 | async-start | bytes 3538944 | tf_op jit(solution)/shard_map/all_gather | solution.py:66
  280.8 11.7 %copy-start.2 = (bf16[64,6144]{1,0:T(8,128)(2,1)S(1)}, bf16[64,6144]{1,0:T(8,128)(2,1)}, u32[]{:S(2)}) copy-start(bf16[64,6144]{1,0:T(8,128)(2,1)} %reduce-scatter.2.cloned.1.call-done) | copy-start | bytes 2359300
  280.8 11.6 %all-to-all-start = ((bf16[8,64,384]{2,1,0:T(8,128)(2,1)}), bf16[8,64,384]{2,1,0:T(8,128)(2,1)S(1)}, u32[]{:S(2)}, u32[]{:S(2)}) async-start(bf16[8,64,384]{2,1,0:T(8,128)(2,1)} %bitcast.6), calls=%async_computation | async-start | bytes 786432 | tf_op jit(solution)/shard_map/all_to_all | solution.py:71
  292.7 31.1 %copy-start.5 = (bf16[512,3072]{1,0:T(8,128)(2,1)S(1)}, bf16[512,3072]{1,0:T(8,128)(2,1)}, u32[]{:S(2)}) copy-start(bf16[512,3072]{1,0:T(8,128)(2,1)} %all-gather.7.cloned.1.call-done) | copy-start | bytes 9437188
  292.7 1.8 collective-permute-start.1
  294.5 11.2 %collective-permute-start.2 = (bf16[64,3072]{1,0:T(8,128)(2,1)S(1)}, bf16[64,3072]{1,0:T(8,128)(2,1)S(1)}, u32[]{:S(2)}, u32[]{:S(2)}) collective-permute-start(bf16[64,3072]{1,0:T(8,128)(2,1)S(1)} %collective-permute-done.1), channel_id=1, source_target_pairs={{0,16},{16,0},{8,24},{24,8},{32,48},{48,32},{40,56},{56,40},{64,80... | collective-permute-start | bytes 1179656 | tf_op jit(solution)/shard_map/ppermute | solution.py:18
  305.7 11.8 %collective-permute-start.3 = (bf16[64,3072]{1,0:T(8,128)(2,1)S(1)}, bf16[64,3072]{1,0:T(8,128)(2,1)S(1)}, u32[]{:S(2)}, u32[]{:S(2)}) collective-permute-start(bf16[64,3072]{1,0:T(8,128)(2,1)S(1)} %collective-permute-done.2), channel_id=1, source_target_pairs={{0,32},{32,0},{8,40},{40,8},{16,48},{48,16},{24,56},{56,24},{64,96... | collective-permute-start | bytes 1179656 | tf_op jit(solution)/shard_map/ppermute | solution.py:18
  317.5 18.8 %collective-permute-start.4 = (bf16[64,3072]{1,0:T(8,128)(2,1)S(1)}, bf16[64,3072]{1,0:T(8,128)(2,1)S(1)}, u32[]{:S(2)}, u32[]{:S(2)}) collective-permute-start(bf16[64,3072]{1,0:T(8,128)(2,1)S(1)} %collective-permute-done.3), channel_id=1, source_target_pairs={{0,64},{64,0},{8,72},{72,8},{16,80},{80,16},{24,88},{88,24},{32,96... | collective-permute-start | bytes 1179656 | tf_op jit(solution)/shard_map/ppermute | solution.py:18
  325.7 67.9 %collective-permute-start.6 = (bf16[64,3072]{1,0:T(8,128)(2,1)S(1)}, bf16[64,3072]{1,0:T(8,128)(2,1)S(1)}, u32[]{:S(2)}, u32[]{:S(2)}) collective-permute-start(bf16[64,3072]{1,0:T(8,128)(2,1)S(1)} %get-tuple-element.9), channel_id=1, source_target_pairs={{8,0},{16,8},{24,16},{32,24},{40,32},{48,40},{56,48},{64,56},{72,6... | collective-permute-start | bytes 1179656 | tf_op jit(solution)/shard_map/ppermute | solution.py:24
  325.8 67.8 %collective-permute-start = (bf16[64,3072]{1,0:T(8,128)(2,1)S(1)}, bf16[64,3072]{1,0:T(8,128)(2,1)S(1)}, u32[]{:S(2)}, u32[]{:S(2)}) collective-permute-start(bf16[64,3072]{1,0:T(8,128)(2,1)S(1)} %get-tuple-element.8), channel_id=1, source_target_pairs={{248,0},{0,8},{8,16},{16,24},{24,32},{32,40},{40,48},{48,56},{56,6... | collective-permute-start | bytes 1179656 | tf_op jit(solution)/shard_map/ppermute | solution.py:24
  336.3 57.3 %collective-permute-start.5 = (bf16[64,3072]{1,0:T(8,128)(2,1)S(1)}, bf16[64,3072]{1,0:T(8,128)(2,1)S(1)}, u32[]{:S(2)}, u32[]{:S(2)}) collective-permute-start(bf16[64,3072]{1,0:T(8,128)(2,1)S(1)} %collective-permute-done.4), channel_id=1, source_target_pairs={{0,128},{128,0},{8,136},{136,8},{16,144},{144,16},{24,152},{152,24... | collective-permute-start | bytes 1179656 | tf_op jit(solution)/shard_map/ppermute | solution.py:18
Sparse Core Ops, SparseCore 0:
  19.2 69.9 all-gather.6
  102.0 76.4 reduce-scatter.1
  182.1 45.3 all-gather.4
  229.2 46.2 all-gather.8
